TPU v7x, 512 devices: a whole 4x4x16 slice. The times are simulated.
512 devices in a mesh: ctx: 64 (over x_hi, z, core), mp: 8 (over x_lo, y).
Axes of the slice: x: 4 (x_hi: 2, x_lo: 2; x = x_hi * 2 + x_lo), y: 4, z: 16, core: 2. Of those that a mesh axis runs over, the one named last changes fastest.
Arguments:
- queries: bfloat16 [4096, 8192], P('ctx', 'mp'), may hold values from -8 to 8
- keys: bfloat16 [4096, 1024], P('ctx', 'mp'), may hold values from -8 to 8
- values: bfloat16 [4096, 1024], P('ctx', 'mp'), may hold values from -6 to 6
- positions: int32 [4096], P('ctx'), may hold values from 0 to 4095, as said below
- x_normed: bfloat16 [4096, 8192], P('ctx', 'mp'), may hold values from -6 to 6
- w_gate: bfloat16 [8192, 16384], P('mp', 'ctx'), may hold values from -0.0625 to 0.0625
- w_up: bfloat16 [8192, 16384], P('mp', 'ctx'), may hold values from -0.0625 to 0.0625
Outputs:
- attended: bfloat16 [4096, 8192], P('ctx', 'mp')
- mlp_hidden: bfloat16 [4096, 16384], P('mp', 'ctx')
Inputs may be any that keep to these rules, and one draw needn't show every extreme that they name: `positions`: each position of 0 to 4095 appears exactly once.
All inputs are finite; a program needn't handle non-finite values.
Results may differ from a plain program's by a relative error of at most 0.02.
Values may be sent and summed in bfloat16 or wider, within the bound.
No kernel may reach another device: no remote copies, remote signals or barrier semaphores. Data moves between devices by JAX's collectives and lax.ppermute only.
A program may use at most 64 MiB of HBM per device.

v0:
```python
import jax
import jax.numpy as jnp
from jax import lax
from jax.sharding import PartitionSpec as P

HEAD = 128


def per_device(queries, keys, values, positions, x_normed, w_gate, w_up):
    tok_rows = queries.shape[0]
    local_heads = queries.shape[1] // HEAD
    local_kv = keys.shape[1] // HEAD
    group = local_heads // local_kv
    scale = HEAD ** (-0.5)
    query_four = queries.reshape(tok_rows, local_kv, group, HEAD)
    top_run = jnp.full((local_kv, group, tok_rows), -1e30, jnp.float32)
    k_piece = lax.all_gather(keys, "ctx", axis=0, tiled=True)
    v_piece = lax.all_gather(values, "ctx", axis=0, tiled=True)
    k_pos = lax.all_gather(positions, "ctx", axis=0, tiled=True)
    count = k_piece.shape[0]
    k_three = k_piece.reshape(count, local_kv, HEAD)
    v_three = v_piece.reshape(count, local_kv, HEAD)
    scores = (
        jnp.einsum("tgjd,sgd->gjts", query_four, k_three, preferred_element_type=jnp.float32)
        * scale
    )
    visible = k_pos[None, :] <= positions[:, None]
    piece_top = jnp.max(jnp.where(visible, scores, jnp.float32(-1e30)), axis=-1)
    top_new = jnp.maximum(top_run, piece_top)
    weights = jnp.where(visible, jnp.exp(scores - top_new[..., None]), jnp.float32(0.0))
    total_new = jnp.sum(weights, axis=-1)
    mixed = jnp.einsum(
        "gjts,sgd->gjtd", weights.astype(jnp.bfloat16), v_three, preferred_element_type=jnp.float32
    )
    final_state = (top_new, total_new, mixed)
    top_run, total_run, accum = final_state
    normed = accum / total_run[..., None]
    attended = (
        jnp.transpose(normed, (2, 0, 1, 3))
        .reshape(tok_rows, local_heads * HEAD)
        .astype(jnp.bfloat16)
    )
    hidden_cols = w_gate.shape[1]
    both_weights = jnp.concatenate((w_gate, w_up), axis=1)
    block_terms = jnp.dot(
        lax.all_gather(x_normed, "ctx", axis=0, tiled=True),
        both_weights,
        preferred_element_type=jnp.float32,
    ).astype(jnp.bfloat16)
    summed = lax.psum_scatter(
        block_terms.astype(jnp.float32).astype(jnp.bfloat16), "mp", scatter_dimension=0, tiled=True
    ).astype(jnp.float32)
    gate = summed[:, :hidden_cols]
    up = summed[:, hidden_cols:]
    mlp_hidden = (jax.nn.silu(gate) * up).astype(jnp.bfloat16)
    return (attended, mlp_hidden)


def solution(mesh):
    return jax.shard_map(
        per_device,
        mesh=mesh,
        in_specs=(
            P("ctx", "mp"),
            P("ctx", "mp"),
            P("ctx", "mp"),
            P("ctx"),
            P("ctx", "mp"),
            P("mp", "ctx"),
            P("mp", "ctx"),
        ),
        out_specs=(P("ctx", "mp"), P("mp", "ctx")),
        check_vma=False,
    )
```

profile of v0, /device:TPU:1, one launch (start us, length us, event | category | flops | bytes accessed | tf_op | source)
XLA Modules:
  0.0 528.0 jit_solution(817598872555930921)
XLA Ops:
  7.2 0.0 copy-start
  7.2 0.0 all-gather.8.cloned.1.call-start
  7.2 0.7 all-gather.8.cloned.1.call-update
  7.9 0.0 all-gather.4.cloned.1.call-start
  8.0 0.7 all-gather.4.cloned.1.call-update
  8.7 0.0 all-gather.6.cloned.1.call-start
  8.7 0.7 all-gather.6.cloned.1.call-update
  9.4 0.0 copy-start.2
  9.4 0.0 reduce-scatter.2.cloned.1.call-start
  9.5 172.6 %all-gather.8.cloned.1.call-done = bf16[4096,1024]{1,0:T(8,128)(2,1)} async-done(((bf16[64,1024]{1,0:T(8,128)(2,1)}), bf16[4096,1024]{1,0:T(8,128)(2,1)}) %all-gather.8.cloned.1.call-update) | async-done | bytes 8388624 | tf_op jit(solution)/shard_map/all_gather | solution.py:46
  182.1 10.2 %fusion.5 = bf16[4096,512]{0,1:T(8,128)(2,1)} fusion(bf16[4096,1024]{1,0:T(8,128)(2,1)} %all-gather.8.cloned.1.call-done, bf16[1024,256]{1,0:T(8,128)(2,1)} %param.13, bf16[1024,256]{1,0:T(8,128)(2,1)} %param.12), kind=kOutput, calls=%fused_computation.8 | convolution fusion | flops 4299161600 | bytes 13631488 | tf_op jit(solution)/shard_map/dot_general | solution.py:45
  192.3 0.0 reduce-scatter.2.cloned.1.call-update
  192.3 1.3 dynamic-slice
  194.3 0.0 copy-done.2
  194.3 0.3 dynamic-update-slice
  194.5 251.6 %all-reduce = s32[4096]{0:T(1024)S(1)} all-reduce(s32[4096]{0:T(1024)S(1)} %dynamic-update-slice), channel_id=1, replica_groups=mesh['ctx'=64,'mp'=8] {'ctx'}, use_global_device_ids=true, to_apply=%add | all-reduce | flops 4096 | bytes 32768
  446.1 0.2 broadcast_compare_fusion
  446.3 0.0 all-gather.4.cloned.1.call-done
  446.4 0.0 copy-done
  446.4 2.9 fusion
  449.3 0.0 copy-start.1
  449.3 3.2 copy-done.1
  452.5 2.4 fusion.3
  454.9 5.6 %all-gather.6.cloned.1.call-done = bf16[4096,128]{1,0:T(8,128)(2,1)} async-done(((bf16[64,128]{1,0:T(8,128)(2,1)}), bf16[4096,128]{1,0:T(8,128)(2,1)}) %all-gather.6.cloned.1.call-update) | async-done | bytes 1048592 | tf_op jit(solution)/shard_map/all_gather | solution.py:18
  460.6 5.2 fusion.16
  465.7 0.1 copy.12
  465.8 0.7 copy.23
  466.5 52.7 %reduce-scatter.2.cloned.1.call-done = bf16[512,512]{0,1:T(8,128)(2,1)} async-done(((bf16[4096,512]{0,1:T(8,128)(2,1)}), bf16[512,512]{0,1:T(8,128)(2,1)}) %reduce-scatter.2.cloned.1.call-update) | async-done | bytes 524304 | tf_op jit(solution)/shard_map/reduce_scatter | solution.py:50
  519.3 1.2 convert_element_type.36
  520.4 0.2 fusion.25
  520.6 0.8 copy.13
  (2 shorter events, 0.0 us)
Async XLA Ops:
  7.2 439.2 %copy-start = (bf16[64,1024]{1,0:T(8,128)(2,1)S(1)}, bf16[64,1024]{1,0:T(8,128)(2,1)}, u32[]{:S(2)}) copy-start(bf16[64,1024]{1,0:T(8,128)(2,1)} %param.7) | copy-start | bytes 393220
  7.2 174.9 %all-gather.8.cloned.1.call-start = ((), (), s32[]{:S(2)}) async-start(), calls=%async_computation.3 | async-start | bytes 8519680 | tf_op jit(solution)/shard_map/all_gather | solution.py:46
  7.9 438.4 %all-gather.4.cloned.1.call-start = ((), (), s32[]{:S(2)}) async-start(), calls=%async_computation.1 | async-start | bytes 1064960 | tf_op jit(solution)/shard_map/all_gather | solution.py:17
  8.7 451.9 %all-gather.6.cloned.1.call-start = ((), (), s32[]{:S(2)}) async-start(), calls=%async_computation.2 | async-start | bytes 1064960 | tf_op jit(solution)/shard_map/all_gather | solution.py:18
  9.4 184.9 %copy-start.2 = (s32[64]{0:T(128)S(1)}, s32[64]{0:T(128)}, u32[]{:S(2)}) copy-start(s32[64]{0:T(128)} %param.10) | copy-start | bytes 772
  9.4 509.9 %reduce-scatter.2.cloned.1.call-start = ((), (), s32[]{:S(2)}) async-start(), calls=%async_computation.4 | async-start | bytes 4718592 | tf_op jit(solution)/shard_map/reduce_scatter | solution.py:50
  449.3 3.2 copy-start.1
Sparse Core Ops, SparseCore 0:
  11.3 170.7 all-gather.7
  185.3 135.2 all-gather.3
  323.9 136.6 all-gather.5
  463.3 55.9 reduce-scatter.1
where the time goes:
time: 528 us
  blocking collectives  252 us (48%)
  waiting for transfers between devices  233 us (44%)
  matrix products  18.3 us (3%)
  between operations  14.5 us (3%)
  local copies, waits for them, and re-layouts  6.38 us (1%)
    unnamed x1, blocking collectives  252 us
    all_gather x1, waiting for transfers between devices, per_device(): lax.all_gather(x_normed, 'ctx', axis=0, tiled=True)  173 us
    reduce_scatter x1, waiting for transfers between devices, per_device(): lax.psum_scatter(block_terms.astype(jnp.float32).astype(jnp.bfloat16), 'm...  52.7 us
  transfers between devices with their start and end apart: 4, of which 3 were waited for; matrix products, arithmetic and copies ran while one was open for 4% of the time, Pallas kernels for 0%

commit v1 on v0

--- a/solution.py
+++ b/solution.py
@@ -43,7 +43,9 @@
     hidden_cols = w_gate.shape[1]
     both_weights = jnp.concatenate((w_gate, w_up), axis=1)
     block_terms = jnp.dot(
-        lax.all_gather(x_normed, "ctx", axis=0, tiled=True),
+        jnp.concatenate(
+            lax.all_to_all(jnp.stack([x_normed] * lax.axis_size("ctx")), "ctx", 0, 0), axis=0
+        ),
         both_weights,
         preferred_element_type=jnp.float32,
     ).astype(jnp.bfloat16)

time: 528 us -> 702 us (1.33)
  waiting for transfers between devices: 233 us -> 373 us
  starting transfers between devices: 0.15 us -> 20 us
    all_to_all x0 -> x1, waiting for transfers between devices: none -> 371 us  [per_device(): lax.all_to_all(jnp.stack([x_normed] * lax.axis_size('ctx')), 'ctx', 0, 0)]
    all_gather x1 -> x0, waiting for transfers between devices: 173 us -> none  [per_device(): lax.all_gather(x_normed, 'ctx', axis=0, tiled=True)]
    reduce_scatter x1, waiting for transfers between devices: 52.7 us -> 0.01 us  [per_device(): lax.psum_scatter(block_terms.astype(jnp.float32).astype(jnp.bfloat16), 'm...]
    all_to_all x0 -> x1, starting transfers between devices: none -> 19.9 us  [per_device(): lax.all_to_all(jnp.stack([x_normed] * lax.axis_size('ctx')), 'ctx', 0, 0)]
  transfers between devices with their start and end apart: 4 -> 4, of which waited for: 3 -> 1; matrix products, arithmetic and copies ran while one was open for 4% -> 3% of each run, Pallas kernels for 0% -> 0%
where the time goes in v1:
time: 702 us; the launch traced here: 697 us
  waiting for transfers between devices  373 us (53%)
  blocking collectives  255 us (36%)
  starting transfers between devices  20 us (3%)
  matrix products  17.6 us (3%)
  between operations  16.2 us (2%)
  local copies, waits for them, and re-layouts  11.6 us (2%)
    all_to_all x1, waiting for transfers between devices, per_device(): lax.all_to_all(jnp.stack([x_normed] * lax.axis_size('ctx')), 'ctx', 0, 0)  371 us
    unnamed x1, blocking collectives  255 us
    all_to_all x1, starting transfers between devices, per_device(): lax.all_to_all(jnp.stack([x_normed] * lax.axis_size('ctx')), 'ctx', 0, 0)  19.9 us
  transfers between devices with their start and end apart: 4, of which 1 were waited for; matrix products, arithmetic and copies ran while one was open for 3% of the time, Pallas kernels for 0%

profile of v1, /device:TPU:1, one launch (start us, length us, event | category | flops | bytes accessed | tf_op | source)
XLA Modules:
  0.0 697.3 jit_solution(9690208061225657952)
XLA Ops:
  8.0 0.0 copy-start
  8.0 5.2 stack.2
  13.2 0.0 copy-start.3
  13.2 0.0 copy-start.4
  13.2 19.9 %all-to-all-start = ((bf16[64,64,1024]{2,1,0:T(8,128)(2,1)}), bf16[64,64,1024]{2,1,0:T(8,128)(2,1)}, u32[]{:S(2)}, u32[]{:S(2)}) async-start(bf16[64,64,1024]{2,1,0:T(8,128)(2,1)} %stack.2), calls=%async_computation | async-start | bytes 16777216 | tf_op jit(solution)/shard_map/all_to_all | solution.py:47
  33.2 0.0 all-gather.3.cloned.1.call-start
  33.2 0.7 all-gather.3.cloned.1.call-update
  33.9 0.0 all-gather.5.cloned.1.call-start
  34.0 0.7 all-gather.5.cloned.1.call-update
  34.7 0.0 reduce-scatter.2.cloned.1.call-start
  34.7 371.5 %all-to-all-done = bf16[64,64,1024]{2,1,0:T(8,128)(2,1)} async-done(((bf16[64,64,1024]{2,1,0:T(8,128)(2,1)}), bf16[64,64,1024]{2,1,0:T(8,128)(2,1)}, u32[]{:S(2)}, u32[]{:S(2)}) %all-to-all-start) | async-done | bytes 8388640 | tf_op jit(solution)/shard_map/all_to_all | solution.py:47
  406.2 0.0 copy-done.3
  406.2 0.0 copy-done.4
  406.2 0.0 copy-start.2
  406.2 9.6 %fusion.5 = bf16[4096,512]{0,1:T(8,128)(2,1)} fusion(bf16[4096,1024]{1,0:T(8,128)(2,1)} %bitcast.9, bf16[1024,256]{1,0:T(8,128)(2,1)S(1)} %copy-done.3, bf16[1024,256]{1,0:T(8,128)(2,1)S(1)} %copy-done.4), kind=kOutput, calls=%fused_computation.8 | convolution fusion | flops 4299161600 | bytes 13631488 | tf_op jit(solution)/shard_map/dot_general | solution.py:45
  415.8 0.0 reduce-scatter.2.cloned.1.call-update
  415.8 1.3 dynamic-slice
  417.7 0.0 copy-done.2
  417.7 0.3 dynamic-update-slice
  418.0 254.9 %all-reduce = s32[4096]{0:T(1024)S(1)} all-reduce(s32[4096]{0:T(1024)S(1)} %dynamic-update-slice), channel_id=1, replica_groups=mesh['ctx'=64,'mp'=8] {'ctx'}, use_global_device_ids=true, to_apply=%add | all-reduce | flops 4096 | bytes 32768
  672.9 0.2 broadcast_compare_fusion
  673.1 0.0 all-gather.3.cloned.1.call-done
  673.1 0.0 copy-done
  673.1 2.9 fusion
  676.0 0.0 copy-start.1
  676.1 3.2 copy-done.1
  679.3 2.4 fusion.3
  681.7 0.0 all-gather.5.cloned.1.call-done
  681.7 5.1 fusion.16
  686.9 0.1 copy.12
  687.0 0.7 copy.23
  687.6 0.0 reduce-scatter.2.cloned.1.call-done
  687.6 1.2 convert_element_type.36
  688.8 0.2 fusion.25
  689.0 0.8 copy.13
  (2 shorter events, 0.0 us)
Async XLA Ops:
  8.0 665.1 %copy-start = (bf16[64,1024]{1,0:T(8,128)(2,1)S(1)}, bf16[64,1024]{1,0:T(8,128)(2,1)}, u32[]{:S(2)}) copy-start(bf16[64,1024]{1,0:T(8,128)(2,1)} %param.7) | copy-start | bytes 393220
  13.2 392.9 %copy-start.3 = (bf16[1024,256]{1,0:T(8,128)(2,1)S(1)}, bf16[1024,256]{1,0:T(8,128)(2,1)}, u32[]{:S(2)}) copy-start(bf16[1024,256]{1,0:T(8,128)(2,1)} %param.13) | copy-start | bytes 1572868
  13.2 392.9 %copy-start.4 = (bf16[1024,256]{1,0:T(8,128)(2,1)S(1)}, bf16[1024,256]{1,0:T(8,128)(2,1)}, u32[]{:S(2)}) copy-start(bf16[1024,256]{1,0:T(8,128)(2,1)} %param.12) | copy-start | bytes 1572868
  13.2 392.9 %all-to-all-start = ((bf16[64,64,1024]{2,1,0:T(8,128)(2,1)}), bf16[64,64,1024]{2,1,0:T(8,128)(2,1)}, u32[]{:S(2)}, u32[]{:S(2)}) async-start(bf16[64,64,1024]{2,1,0:T(8,128)(2,1)} %stack.2), calls=%async_computation | async-start | bytes 16777216 | tf_op jit(solution)/shard_map/all_to_all | solution.py:47
  33.2 640.0 %all-gather.3.cloned.1.call-start = ((), (), s32[]{:S(2)}) async-start(), calls=%async_computation.2 | async-start | bytes 1064960 | tf_op jit(solution)/shard_map/all_gather | solution.py:17
  33.9 647.8 %all-gather.5.cloned.1.call-start = ((), (), s32[]{:S(2)}) async-start(), calls=%async_computation.3 | async-start | bytes 1064960 | tf_op jit(solution)/shard_map/all_gather | solution.py:18
  34.7 653.0 %reduce-scatter.2.cloned.1.call-start = ((), (), s32[]{:S(2)}) async-start(), calls=%async_computation.4 | async-start | bytes 4718592 | tf_op jit(solution)/shard_map/reduce_scatter | solution.py:52
  406.2 11.5 %copy-start.2 = (s32[64]{0:T(128)S(1)}, s32[64]{0:T(128)}, u32[]{:S(2)}) copy-start(s32[64]{0:T(128)} %param.10) | copy-start | bytes 772
  676.0 3.2 copy-start.1
Sparse Core Ops, SparseCore 0:
  37.3 156.0 all-gather.2
  196.7 161.1 all-gather.4
Sparse Core Ops, SparseCore 1:
  415.9 57.6 reduce-scatter.1
